TPU v7x, 32 devices: a whole 2x2x4 slice. The times are simulated.
32 devices in a mesh: row: 4 (over z), col: 8 (over y, x, core).
Axes of the slice: x: 2, y: 2, z: 4, core: 2. Of those that a mesh axis runs over, the one named last changes fastest.
Arguments:
- layer_input: bfloat16 [8192, 2048], P(('col', 'row')), may hold values from -6 to 6
- w_query: bfloat16 [2048, 2048], P('col', 'row'), may hold values from -0.125 to 0.125
- w_key: bfloat16 [2048, 2048], P('col', 'row'), may hold values from -0.125 to 0.125
- w_value: bfloat16 [2048, 2048], P('col', 'row'), may hold values from -0.125 to 0.125
- w_output: bfloat16 [2048, 2048], P('row', 'col'), may hold values from -1.5 to 1.5
- w_gate: bfloat16 [2048, 8192], P('col', 'row'), may hold values from -0.125 to 0.125
- w_up: bfloat16 [2048, 8192], P('col', 'row'), may hold values from -0.125 to 0.125
- w_down: bfloat16 [8192, 2048], P('row', 'col'), may hold values from -0.0625 to 0.0625
- piece_starts: int32 [8, 2], P('col'), may hold values from 0 to 768, as said below
- cotangent: bfloat16 [8192, 2048], P(('col', 'row')), may hold values from -6 to 6
Outputs:
- output: bfloat16 [8192, 2048], P(('col', 'row'))
- input_grad: float32 [8192, 2048], P(('col', 'row'))
- grad_w_query: float32 [2048, 2048], P('col', 'row')
- grad_w_key: float32 [2048, 2048], P('col', 'row')
- grad_w_value: float32 [2048, 2048], P('col', 'row')
- grad_w_output: float32 [2048, 2048], P('row', 'col')
- grad_w_gate: float32 [2048, 8192], P('col', 'row')
- grad_w_up: float32 [2048, 8192], P('col', 'row')
- grad_w_down: float32 [8192, 2048], P('row', 'col')
Inputs may be any that keep to these rules, and one draw needn't show every extreme that they name: `piece_starts`: piece p of a sequence starts at p * 512 or later and ends by (p + 1) * 512, so the pieces of one sequence do not intersect.
All inputs are finite; a program needn't handle non-finite values.
Results may differ from a plain program's by a relative error of at most 0.019.
Values may be sent and summed in bfloat16 or wider, within the bound.
No kernel may reach another device: no remote copies, remote signals or barrier semaphores. Data moves between devices by JAX's collectives and lax.ppermute only.
A program may use at most 256 MiB of HBM per device.

v0:
```python
import math
import jax
import jax.numpy as jnp
from jax import lax
from jax.sharding import PartitionSpec as P

HD = 128
LENGTH = 1024
PIECE = 256
EPSILON = 1e-05
NEGATIVE = -1e30


def product(left, right):
    return jnp.dot(left, right, preferred_element_type=jnp.float32)


def contract_rows(left, right):
    return lax.dot_general(
        left, right, (((0,), (0,)), ((), ())), preferred_element_type=jnp.float32
    )


def times_transpose(left, right):
    return lax.dot_general(
        left, right, (((1,), (1,)), ((), ())), preferred_element_type=jnp.float32
    )


def layer_norm(inputs):
    center = inputs - jnp.mean(inputs, axis=-1, keepdims=True)
    spread = jnp.mean(center * center, axis=-1, keepdims=True)
    return center * lax.rsqrt(spread + EPSILON)


def norm_back(inputs, grad):
    center = inputs - jnp.mean(inputs, axis=-1, keepdims=True)
    inverse = lax.rsqrt(jnp.mean(center * center, axis=-1, keepdims=True) + EPSILON)
    normed = center * inverse
    return inverse * (
        grad
        - jnp.mean(grad, axis=-1, keepdims=True)
        - normed * jnp.mean(grad * normed, axis=-1, keepdims=True)
    )


def rope_tables():
    positions = jnp.arange(LENGTH, dtype=jnp.float32)
    freqs = jnp.power(jnp.float32(10000.0), -jnp.arange(HD // 2, dtype=jnp.float32) * (2.0 / HD))
    angles = positions[:, None] * freqs[None, :]
    return (jnp.cos(angles)[:, None, :], jnp.sin(angles)[:, None, :])


def rotate(field, cosine, sine):
    half_size = field.shape[-1] // 2
    first_half = field[..., :half_size]
    second_half = field[..., half_size:]
    return jnp.concatenate(
        [first_half * cosine - second_half * sine, second_half * cosine + first_half * sine],
        axis=-1,
    )


def unrotate(field, cosine, sine):
    half_size = field.shape[-1] // 2
    first_half = field[..., :half_size]
    second_half = field[..., half_size:]
    return jnp.concatenate(
        [first_half * cosine + second_half * sine, second_half * cosine - first_half * sine],
        axis=-1,
    )


def piece_mask(starts):
    positions = jnp.arange(LENGTH, dtype=jnp.int32)
    inside = (positions[None, :] >= starts[:, None]) & (
        positions[None, :] < starts[:, None] + PIECE
    )
    shared = jnp.any(inside[:, :, None] & inside[:, None, :], axis=0)
    causal = positions[None, :] <= positions[:, None]
    return causal | shared


def masked_scores(queries, keys_rot, starts):
    scale = 1.0 / math.sqrt(HD)
    scores = (
        jnp.einsum("qhd,khd->hqk", queries, keys_rot, preferred_element_type=jnp.float32) * scale
    )
    return jnp.where(piece_mask(starts)[None], scores, NEGATIVE)


def attend_forward(operands):
    queries, keys_rot, values, starts = operands
    scores = masked_scores(queries, keys_rot, starts)
    row_top = jnp.max(scores, axis=-1, keepdims=True)
    shifted = jnp.exp(scores - row_top)
    row_total = jnp.sum(shifted, axis=-1, keepdims=True)
    probs = (shifted / row_total).astype(jnp.bfloat16)
    mixed = jnp.einsum("hqk,khd->qhd", probs, values, preferred_element_type=jnp.float32)
    return (mixed, row_top + jnp.log(row_total))


def attend_backward(operands):
    queries, keys_rot, values, starts, log_total, grad_mixed = operands
    scale = 1.0 / math.sqrt(HD)
    scores = masked_scores(queries, keys_rot, starts)
    probs = jnp.exp(scores - log_total)
    probs_low = probs.astype(jnp.bfloat16)
    grad_values = jnp.einsum(
        "hqk,qhd->khd", probs_low, grad_mixed, preferred_element_type=jnp.float32
    )
    grad_probs = jnp.einsum("qhd,khd->hqk", grad_mixed, values, preferred_element_type=jnp.float32)
    inner = jnp.sum(probs * grad_probs, axis=-1, keepdims=True)
    grad_scores = (probs * (grad_probs - inner)).astype(jnp.bfloat16)
    grad_queries = (
        jnp.einsum("hqk,khd->qhd", grad_scores, keys_rot, preferred_element_type=jnp.float32)
        * scale
    )
    grad_keys = (
        jnp.einsum("hqk,qhd->khd", grad_scores, queries, preferred_element_type=jnp.float32) * scale
    )
    return (grad_queries, grad_keys, grad_values)


def per_device(
    layer_input, w_query, w_key, w_value, w_output, w_gate, w_up, w_down, piece_starts, cotangent
):
    seq_count = piece_starts.shape[0]
    group_rows = seq_count * LENGTH
    heads_local = w_query.shape[1] // HD
    gathered = (
        lax.all_gather(w_query, "col", axis=0, tiled=True),
        lax.all_gather(w_key, "col", axis=0, tiled=True),
        lax.all_gather(w_value, "col", axis=0, tiled=True),
        lax.all_gather(w_output, "col", axis=1, tiled=True),
        lax.all_gather(w_gate, "col", axis=0, tiled=True),
        lax.all_gather(w_up, "col", axis=0, tiled=True),
        lax.all_gather(w_down, "col", axis=1, tiled=True),
    )
    full_query, full_key, full_value, full_output, full_gate, full_up, full_down = gathered
    cosine, sine = rope_tables()
    inputs = layer_input.astype(jnp.float32)
    normed_first = layer_norm(inputs).astype(jnp.bfloat16)
    first_rows = lax.all_gather(normed_first, "row", axis=0, tiled=True)

    def split_heads(matrix):
        return matrix.reshape(seq_count, LENGTH, heads_local, HD)

    def merge_heads(field):
        return field.reshape(group_rows, heads_local * HD)

    queries = rotate(split_heads(product(first_rows, full_query)), cosine, sine).astype(
        jnp.bfloat16
    )
    keys_rot = rotate(split_heads(product(first_rows, full_key)), cosine, sine).astype(jnp.bfloat16)
    values = split_heads(product(first_rows, full_value)).astype(jnp.bfloat16)
    mixed, log_total = lax.map(attend_forward, (queries, keys_rot, values, piece_starts))
    attended = merge_heads(mixed.astype(jnp.bfloat16))
    attention_sum = lax.psum_scatter(
        product(attended, full_output), "row", scatter_dimension=0, tiled=True
    )
    middle = inputs + attention_sum
    normed_second = layer_norm(middle).astype(jnp.bfloat16)
    second_rows = lax.all_gather(normed_second, "row", axis=0, tiled=True)
    gate_lin = product(second_rows, full_gate)
    up_lin = product(second_rows, full_up)
    activation = (jax.nn.silu(gate_lin) * up_lin).astype(jnp.bfloat16)
    ffn_sum = lax.psum_scatter(
        product(activation, full_down).astype(jnp.bfloat16), "row", scatter_dimension=0, tiled=True
    ).astype(jnp.float32)
    output = (middle + ffn_sum).astype(jnp.bfloat16)
    back_query, back_key, back_value, back_output = (full_query, full_key, full_value, full_output)
    back_gate, back_up, back_down = (full_gate, full_up, full_down)
    grad_rows = lax.all_gather(cotangent, "row", axis=0, tiled=True)
    grad_activation = times_transpose(grad_rows, back_down)
    sigma = jax.nn.sigmoid(gate_lin)
    grad_gate = (grad_activation * up_lin * sigma * (1.0 + gate_lin * (1.0 - sigma))).astype(
        jnp.bfloat16
    )
    grad_up = (grad_activation * gate_lin * sigma).astype(jnp.bfloat16)
    grad_second = lax.psum_scatter(
        (times_transpose(grad_gate, back_gate) + times_transpose(grad_up, back_up)).astype(
            jnp.bfloat16
        ),
        "row",
        scatter_dimension=0,
        tiled=True,
    ).astype(jnp.float32)
    grad_middle = cotangent.astype(jnp.float32) + norm_back(middle, grad_second)
    grad_branch = lax.all_gather(grad_middle.astype(jnp.bfloat16), "row", axis=0, tiled=True)
    grad_mixed = split_heads(times_transpose(grad_branch, back_output).astype(jnp.bfloat16))
    grad_q_rot, grad_k_rot, grad_values = lax.map(
        attend_backward, (queries, keys_rot, values, piece_starts, log_total, grad_mixed)
    )
    grad_query = merge_heads(unrotate(grad_q_rot, cosine, sine)).astype(jnp.bfloat16)
    grad_key = merge_heads(unrotate(grad_k_rot, cosine, sine)).astype(jnp.bfloat16)
    grad_value = merge_heads(grad_values).astype(jnp.bfloat16)
    grad_first = lax.psum_scatter(
        (
            times_transpose(grad_query, back_query)
            + times_transpose(grad_key, back_key)
            + times_transpose(grad_value, back_value)
        ).astype(jnp.bfloat16),
        "row",
        scatter_dimension=0,
        tiled=True,
    ).astype(jnp.float32)
    grad_input = grad_middle + norm_back(inputs, grad_first)
    grad_query_w = contract_rows(first_rows, grad_query)
    grad_key_w = contract_rows(first_rows, grad_key)
    grad_value_w = contract_rows(first_rows, grad_value)
    grad_output_w = contract_rows(attended, grad_branch)
    grad_gate_w = contract_rows(second_rows, grad_gate)
    grad_up_w = contract_rows(second_rows, grad_up)
    grad_down_w = contract_rows(activation, grad_rows)
    summed = (
        lax.psum_scatter(
            grad_query_w.astype(jnp.bfloat16), "col", scatter_dimension=0, tiled=True
        ).astype(jnp.float32),
        lax.psum_scatter(
            grad_key_w.astype(jnp.bfloat16), "col", scatter_dimension=0, tiled=True
        ).astype(jnp.float32),
        lax.psum_scatter(
            grad_value_w.astype(jnp.bfloat16), "col", scatter_dimension=0, tiled=True
        ).astype(jnp.float32),
        lax.psum_scatter(
            grad_output_w.astype(jnp.bfloat16), "col", scatter_dimension=1, tiled=True
        ).astype(jnp.float32),
        lax.psum_scatter(
            grad_gate_w.astype(jnp.bfloat16), "col", scatter_dimension=0, tiled=True
        ).astype(jnp.float32),
        lax.psum_scatter(
            grad_up_w.astype(jnp.bfloat16), "col", scatter_dimension=0, tiled=True
        ).astype(jnp.float32),
        lax.psum_scatter(
            grad_down_w.astype(jnp.bfloat16), "col", scatter_dimension=1, tiled=True
        ).astype(jnp.float32),
    )
    results = tuple(summed)
    return (
        output,
        grad_input,
        results[0],
        results[1],
        results[2],
        results[3],
        results[4],
        results[5],
        results[6],
    )


def solution(mesh):
    in_specs = (
        P(("col", "row"), None),
        P("col", "row"),
        P("col", "row"),
        P("col", "row"),
        P("row", "col"),
        P("col", "row"),
        P("col", "row"),
        P("row", "col"),
        P("col", None),
        P(("col", "row"), None),
    )
    out_specs = (
        P(("col", "row"), None),
        P(("col", "row"), None),
        P("col", "row"),
        P("col", "row"),
        P("col", "row"),
        P("row", "col"),
        P("col", "row"),
        P("col", "row"),
        P("row", "col"),
    )
    return jax.shard_map(
        per_device, mesh=mesh, in_specs=in_specs, out_specs=out_specs, check_vma=False
    )
```

profile of v0, /device:TPU:0, one launch (start us, length us, event | category | flops | bytes accessed | tf_op | source)
XLA Modules:
  0.0 1478.2 jit_solution(13351820157895669522)
XLA Ops:
  11.7 2.5 fusion.10
  18.2 2.6 copy.49
  20.8 1.9 fusion.30
  22.8 17.7 %all-gather.18.cloned.1.call-done = bf16[2048,512]{1,0:T(8,128)(2,1)} async-done(((bf16[256,512]{1,0:T(8,128)(2,1)}), bf16[2048,512]{1,0:T(8,128)(2,1)}) %all-gather.18.cloned.1.call-update) | async-done | bytes 2097168 | tf_op jit(solution)/shard_map/all_gather | solution.py:133
  40.4 82.9 %all-gather.12.cloned.1.call-done = bf16[1024,2048]{1,0:T(8,128)(2,1)} async-done(((bf16[256,2048]{1,0:T(8,128)(2,1)}), bf16[1024,2048]{1,0:T(8,128)(2,1)}) %all-gather.12.cloned.1.call-update) | async-done | bytes 4194320 | tf_op jit(solution)/shard_map/all_gather | solution.py:144
  123.3 5.2 fusion.41
  132.0 3.2 copy.78
  135.2 16.4 %all-gather.16.cloned.1.call-done = bf16[2048,512]{1,0:T(8,128)(2,1)} async-done(((bf16[256,512]{1,0:T(8,128)(2,1)}), bf16[2048,512]{1,0:T(8,128)(2,1)}) %all-gather.16.cloned.1.call-update) | async-done | bytes 2097168 | tf_op jit(solution)/shard_map/all_gather | solution.py:132
  151.5 5.2 fusion.40
  158.3 3.2 copy.77
  161.5 3.2 copy.76
  164.6 4.0 fusion.25
  170.7 8.5 fusion.39
  179.2 1.9 all-gather.14.cloned.1.call-done
  181.1 5.2 convolution_convert_fusion.9
  186.3 8.6 fusion
  195.6 7.6 fusion.21
  203.2 7.8 all-gather.20.cloned.1.call-done
  210.9 7.2 fusion.42
  219.0 144.0 %reduce-scatter.12.cloned.1.call-done = f32[256,2048]{1,0:T(8,128)} async-done(((f32[1024,2048]{1,0:T(8,128)}), f32[256,2048]{1,0:T(8,128)}) %reduce-scatter.12.cloned.1.call-update) | async-done | bytes 2097168 | tf_op jit(solution)/shard_map/reduce_scatter | solution.py:159
  363.0 1.9 fusion.36
  368.6 51.1 %all-gather.26.cloned.1.call-done = bf16[2048,2048]{1,0:T(8,128)(2,1)} async-done(((bf16[256,2048]{1,0:T(8,128)(2,1)}), bf16[2048,2048]{1,0:T(8,128)(2,1)}) %all-gather.26.cloned.1.call-update) | async-done | bytes 8388624 | tf_op jit(solution)/shard_map/all_gather | solution.py:137
  419.7 82.9 %all-gather.22.cloned.1.call-done = bf16[1024,2048]{1,0:T(8,128)(2,1)} async-done(((bf16[256,2048]{1,0:T(8,128)(2,1)}), bf16[1024,2048]{1,0:T(8,128)(2,1)}) %all-gather.22.cloned.1.call-update) | async-done | bytes 4194320 | tf_op jit(solution)/shard_map/all_gather | solution.py:164
  502.6 14.7 fusion.44
  517.3 40.0 %all-gather.24.cloned.1.call-done = bf16[2048,2048]{1,0:T(8,128)(2,1)} async-done(((bf16[256,2048]{1,0:T(8,128)(2,1)}), bf16[2048,2048]{1,0:T(8,128)(2,1)}) %all-gather.24.cloned.1.call-update) | async-done | bytes 8388624 | tf_op jit(solution)/shard_map/all_gather | solution.py:136
  557.3 14.5 fusion.43
  571.8 67.7 %all-gather.30.cloned.1.call-done = bf16[1024,2048]{1,0:T(8,128)(2,1)} async-done(((bf16[256,2048]{1,0:T(8,128)(2,1)}), bf16[1024,2048]{1,0:T(8,128)(2,1)}) %all-gather.30.cloned.1.call-update) | async-done | bytes 4194320 | tf_op jit(solution)/shard_map/all_gather | solution.py:174
  639.5 56.3 %all-gather.28.cloned.1.call-done = bf16[2048,2048]{1,0:T(8,128)(2,1)} async-done(((bf16[2048,256]{1,0:T(8,128)(2,1)}), bf16[2048,2048]{1,0:T(8,128)(2,1)}) %all-gather.28.cloned.1.call-update) | async-done | bytes 8388624 | tf_op jit(solution)/shard_map/all_gather | solution.py:138
  695.8 21.8 %multiply_convert_fusion.1 = (bf16[1024,2048]{1,0:T(8,128)(2,1)}, bf16[1024,2048]{1,0:T(8,128)(2,1)}, bf16[1024,2048]{1,0:T(8,128)(2,1)}) fusion(f32[1024,2048]{1,0:T(8,128)} %fusion.43, f32[1024,2048]{1,0:T(8,128)} %fusion.44, bf16[1024,2048]{1,0:T(8,128)(2,1)} %all-gather.30.cloned.1.call-done, bf16[2048,2048]{1,0:T(8,128)(2,1)} %all-gather.28.cloned.1.call-done), kind=kOutput, calls=%fused_computation.12 | convolution fusion | flops 8623489024 | bytes 41943040 | tf_op jit(solution)/shard_map/dot_general | solution.py:25
  717.6 13.1 fusion.45
  730.8 12.9 add_convert_fusion.1
  743.8 13.9 convolution_convert_fusion.3
  757.9 62.7 %reduce-scatter.16.cloned.1.call-done = bf16[256,2048]{1,0:T(8,128)(2,1)} async-done(((bf16[1024,2048]{1,0:T(8,128)(2,1)}), bf16[256,2048]{1,0:T(8,128)(2,1)}) %reduce-scatter.16.cloned.1.call-update) | async-done | bytes 1048592 | tf_op jit(solution)/shard_map/reduce_scatter | solution.py:181
  822.5 77.8 %reduce-scatter.14.cloned.1.call-done = bf16[256,2048]{1,0:T(8,128)(2,1)} async-done(((bf16[1024,2048]{1,0:T(8,128)(2,1)}), bf16[256,2048]{1,0:T(8,128)(2,1)}) %reduce-scatter.14.cloned.1.call-update) | async-done | bytes 1048592 | tf_op jit(solution)/shard_map/reduce_scatter | solution.py:168
  900.3 4.6 fusion.34
  905.0 14.1 convolution_convert_fusion.1
  919.1 14.1 convolution_convert_fusion.2
  933.5 14.1 convolution_convert_fusion
  948.3 38.0 %all-gather.32.cloned.1.call-done = bf16[1024,2048]{1,0:T(8,128)(2,1)} async-done(((bf16[256,2048]{1,0:T(8,128)(2,1)}), bf16[1024,2048]{1,0:T(8,128)(2,1)}) %all-gather.32.cloned.1.call-update) | async-done | bytes 4194320 | tf_op jit(solution)/shard_map/all_gather | solution.py:190
  986.3 5.9 convolution_convert_fusion.4
  992.7 5.9 convolution_convert_fusion.8
  998.6 10.9 fusion.22
  1010.5 3.8 convolution_convert_fusion.5
  1014.3 11.0 multiply_reduce_fusion
  1025.5 12.6 multiply_convert_fusion
  1038.1 3.4 multiply_bitcast_fusion.1
  1041.6 2.4 multiply_bitcast_fusion
  1047.4 6.3 convolution_convert_fusion.7
  1055.1 6.4 convolution_convert_fusion.6
  1061.6 4.5 fusion.47
  1066.1 2.4 fusion.46
  1068.5 6.4 add_convert_fusion
  1074.9 2.9 convert_element_type.182
  1077.8 56.7 %reduce-scatter.28.cloned.1.call-done = bf16[256,2048]{1,0:T(8,128)(2,1)} async-done(((bf16[2048,2048]{1,0:T(8,128)(2,1)}), bf16[256,2048]{1,0:T(8,128)(2,1)}) %reduce-scatter.28.cloned.1.call-update) | async-done | bytes 1048592 | tf_op jit(solution)/shard_map/reduce_scatter | solution.py:229
  1134.5 2.8 convert_element_type.180
  1137.3 71.8 %reduce-scatter.32.cloned.1.call-done = bf16[2048,256]{1,0:T(8,128)(2,1)} async-done(((bf16[2048,2048]{1,0:T(8,128)(2,1)}), bf16[2048,256]{1,0:T(8,128)(2,1)}) %reduce-scatter.32.cloned.1.call-update) | async-done | bytes 1048592 | tf_op jit(solution)/shard_map/reduce_scatter | solution.py:235
  1209.1 2.7 convert_element_type.184
  1211.8 41.6 %reduce-scatter.26.cloned.1.call-done = bf16[512,256]{1,0:T(8,128)(2,1)} async-done(((bf16[512,2048]{1,0:T(8,128)(2,1)}), bf16[512,256]{1,0:T(8,128)(2,1)}) %reduce-scatter.26.cloned.1.call-update) | async-done | bytes 262160 | tf_op jit(solution)/shard_map/reduce_scatter | solution.py:226
  1255.2 42.6 %reduce-scatter.24.cloned.1.call-done = bf16[256,512]{1,0:T(8,128)(2,1)} async-done(((bf16[2048,512]{1,0:T(8,128)(2,1)}), bf16[256,512]{1,0:T(8,128)(2,1)}) %reduce-scatter.24.cloned.1.call-update) | async-done | bytes 262160 | tf_op jit(solution)/shard_map/reduce_scatter | solution.py:223
  1299.7 42.5 %reduce-scatter.20.cloned.1.call-done = bf16[256,512]{1,0:T(8,128)(2,1)} async-done(((bf16[2048,512]{1,0:T(8,128)(2,1)}), bf16[256,512]{1,0:T(8,128)(2,1)}) %reduce-scatter.20.cloned.1.call-update) | async-done | bytes 262160 | tf_op jit(solution)/shard_map/reduce_scatter | solution.py:217
  1343.9 42.6 %reduce-scatter.22.cloned.1.call-done = bf16[256,512]{1,0:T(8,128)(2,1)} async-done(((bf16[2048,512]{1,0:T(8,128)(2,1)}), bf16[256,512]{1,0:T(8,128)(2,1)}) %reduce-scatter.22.cloned.1.call-update) | async-done | bytes 262160 | tf_op jit(solution)/shard_map/reduce_scatter | solution.py:220
  1388.4 77.3 %reduce-scatter.18.cloned.1.call-done = bf16[256,2048]{1,0:T(8,128)(2,1)} async-done(((bf16[1024,2048]{1,0:T(8,128)(2,1)}), bf16[256,2048]{1,0:T(8,128)(2,1)}) %reduce-scatter.18.cloned.1.call-update) | async-done | bytes 1048592 | tf_op jit(solution)/shard_map/reduce_scatter | solution.py:198
  1465.7 1.9 convert_reduce_fusion
  1467.6 3.3 fusion.13
  (149 shorter events, 37.4 us)
Async XLA Ops:
  7.2 9.0 copy-start.31
  7.2 33.2 %all-gather.18.cloned.1.call-start = ((), (), s32[]{:S(2)}) async-start(), calls=%async_computation.14 | async-start | bytes 2359296 | tf_op jit(solution)/shard_map/all_gather | solution.py:133
  7.9 115.4 %all-gather.12.cloned.1.call-start = ((), (), s32[]{:S(2)}) async-start(), calls=%async_computation.11 | async-start | bytes 5242880 | tf_op jit(solution)/shard_map/all_gather | solution.py:144
  9.4 1.7 copy-start.27
  11.1 0.6 copy-start.29
  14.2 137.3 %all-gather.16.cloned.1.call-start = ((), (), s32[]{:S(2)}) async-start(), calls=%async_computation.13 | async-start | bytes 2359296 | tf_op jit(solution)/shard_map/all_gather | solution.py:132
  15.0 166.1 %all-gather.14.cloned.1.call-start = ((), (), s32[]{:S(2)}) async-start(), calls=%async_computation.12 | async-start | bytes 2359296 | tf_op jit(solution)/shard_map/all_gather | solution.py:134
  15.5 195.4 %all-gather.20.cloned.1.call-start = ((), (), s32[]{:S(2)}) async-start(), calls=%async_computation.15 | async-start | bytes 2359296 | tf_op jit(solution)/shard_map/all_gather | solution.py:135
  16.1 346.8 %reduce-scatter.12.cloned.1.call-start = ((), (), s32[]{:S(2)}) async-start(), calls=%async_computation.16 | async-start | bytes 10485760 | tf_op jit(solution)/shard_map/reduce_scatter | solution.py:159
  22.7 141.9 %copy-start.3 = (f32[1024,64]{1,0:T(8,128)}, f32[1024,64]{1,0:T(8,128)S(1)}, u32[]{:S(2)}) copy-start(f32[1024,64]{1,0:T(8,128)S(1)} %get-tuple-element.88) | copy-start | bytes 786436
  22.7 141.9 %copy-start.5 = (f32[1024,64]{1,0:T(8,128)}, f32[1024,64]{1,0:T(8,128)S(1)}, u32[]{:S(2)}) copy-start(f32[1024,64]{1,0:T(8,128)S(1)} %get-tuple-element.89) | copy-start | bytes 786436
  164.6 6.0 copy-start.16
  168.7 1.0 copy-start.8
  168.7 1.3 copy-start.10
  168.7 1.6 copy-start.19
  168.7 2.0 copy-start.21
  179.2 15.8 %copy-start.23 = (f32[4,1024]{1,0:T(4,128)}, f32[4,1024]{1,0:T(4,128)S(1)}, u32[]{:S(2)}) copy-start(f32[4,1024]{1,0:T(4,128)S(1)} %get-tuple-element.90) | copy-start | bytes 49156
  186.3 8.7 copy-start.14
  195.0 0.6 copy-start.25
  203.2 15.0 %copy-start.34 = (bf16[4,128,1024]{2,1,0:T(8,128)(2,1)}, bf16[4,128,1024]{2,1,0:T(8,128)(2,1)S(1)}, u32[]{:S(2)}) copy-start(bf16[4,128,1024]{2,1,0:T(8,128)(2,1)S(1)} %fusion.21) | copy-start | bytes 3145732
  218.2 144.8 %copy-start = (bf16[256,2048]{1,0:T(8,128)(2,1)S(1)}, bf16[256,2048]{1,0:T(8,128)(2,1)}, u32[]{:S(2)}) copy-start(bf16[256,2048]{1,0:T(8,128)(2,1)} %param.10) | copy-start | bytes 3145732
  218.2 201.6 %all-gather.26.cloned.1.call-start = ((), (), s32[]{:S(2)}) async-start(), calls=%async_computation.19 | async-start | bytes 9437184 | tf_op jit(solution)/shard_map/all_gather | solution.py:137
  218.9 283.7 %all-gather.22.cloned.1.call-start = ((), (), s32[]{:S(2)}) async-start(), calls=%async_computation.17 | async-start | bytes 5242880 | tf_op jit(solution)/shard_map/all_gather | solution.py:164
  366.5 190.8 %all-gather.24.cloned.1.call-start = ((), (), s32[]{:S(2)}) async-start(), calls=%async_computation.18 | async-start | bytes 9437184 | tf_op jit(solution)/shard_map/all_gather | solution.py:136
  367.2 272.3 %all-gather.30.cloned.1.call-start = ((), (), s32[]{:S(2)}) async-start(), calls=%async_computation.22 | async-start | bytes 5242880 | tf_op jit(solution)/shard_map/all_gather | solution.py:174
  367.8 327.9 %all-gather.28.cloned.1.call-start = ((), (), s32[]{:S(2)}) async-start(), calls=%async_computation.20 | async-start | bytes 9437184 | tf_op jit(solution)/shard_map/all_gather | solution.py:138
  368.6 452.1 %reduce-scatter.16.cloned.1.call-start = ((), (), s32[]{:S(2)}) async-start(), calls=%async_computation.23 | async-start | bytes 5242880 | tf_op jit(solution)/shard_map/reduce_scatter | solution.py:181
  717.6 13.2 copy-start.36
  743.7 156.6 %reduce-scatter.14.cloned.1.call-start = ((), (), s32[]{:S(2)}) async-start(), calls=%async_computation.21 | async-start | bytes 5242880 | tf_op jit(solution)/shard_map/reduce_scatter | solution.py:168
  757.7 142.6 %copy-start.7 = (bf16[256,2048]{1,0:T(8,128)(2,1)S(1)}, bf16[256,2048]{1,0:T(8,128)(2,1)}, u32[]{:S(2)}) copy-start(bf16[256,2048]{1,0:T(8,128)(2,1)} %param.19) | copy-start | bytes 3145732
  757.7 228.7 %all-gather.32.cloned.1.call-start = ((), (), s32[]{:S(2)}) async-start(), calls=%async_computation.24 | async-start | bytes 5242880 | tf_op jit(solution)/shard_map/all_gather | solution.py:190
  904.9 170.0 %reduce-scatter.30.cloned.1.call-start = ((), (), s32[]{:S(2)}) async-start(), calls=%async_computation.31 | async-start | bytes 9437184 | tf_op jit(solution)/shard_map/reduce_scatter | solution.py:232
  919.1 215.4 %reduce-scatter.28.cloned.1.call-start = ((), (), s32[]{:S(2)}) async-start(), calls=%async_computation.30 | async-start | bytes 9437184 | tf_op jit(solution)/shard_map/reduce_scatter | solution.py:229
  933.3 275.9 %reduce-scatter.32.cloned.1.call-start = ((), (), s32[]{:S(2)}) async-start(), calls=%async_computation.32 | async-start | bytes 9437184 | tf_op jit(solution)/shard_map/reduce_scatter | solution.py:235
  947.6 0.7 copy-start.24
  947.6 0.7 copy-start.26
  947.6 38.8 %copy-start.35 = (bf16[4,128,1024]{2,1,0:T(8,128)(2,1)S(1)}, bf16[4,128,1024]{2,1,0:T(8,128)(2,1)}, u32[]{:S(2)}) copy-start(bf16[4,128,1024]{2,1,0:T(8,128)(2,1)} %copy-done.34) | copy-start | bytes 3145732
  947.6 305.8 %reduce-scatter.26.cloned.1.call-start = ((), (), s32[]{:S(2)}) async-start(), calls=%async_computation.29 | async-start | bytes 2359296 | tf_op jit(solution)/shard_map/reduce_scatter | solution.py:226
  992.3 305.6 %reduce-scatter.24.cloned.1.call-start = ((), (), s32[]{:S(2)}) async-start(), calls=%async_computation.28 | async-start | bytes 2359296 | tf_op jit(solution)/shard_map/reduce_scatter | solution.py:223
  998.6 11.9 copy-start.32
  1009.5 1.0 copy-start.12
  1010.5 3.8 copy-start.15
  1025.3 316.9 %reduce-scatter.20.cloned.1.call-start = ((), (), s32[]{:S(2)}) async-start(), calls=%async_computation.26 | async-start | bytes 2359296 | tf_op jit(solution)/shard_map/reduce_scatter | solution.py:217
  1025.5 12.6 copy-start.9
  1025.5 12.6 copy-start.11
  1038.1 3.4 copy-start.20
  1038.1 3.4 copy-start.22
  1041.6 2.4 copy-start.4
  1041.6 2.4 copy-start.6
  1053.7 332.9 %reduce-scatter.22.cloned.1.call-start = ((), (), s32[]{:S(2)}) async-start(), calls=%async_computation.27 | async-start | bytes 2359296 | tf_op jit(solution)/shard_map/reduce_scatter | solution.py:220
  1055.1 6.4 copy-start.18
  1061.5 4.5 copy-start.17
  1061.5 404.2 %reduce-scatter.18.cloned.1.call-start = ((), (), s32[]{:S(2)}) async-start(), calls=%async_computation.25 | async-start | bytes 5242880 | tf_op jit(solution)/shard_map/reduce_scatter | solution.py:198
  1061.6 4.5 copy-start.33
  1066.0 2.4 copy-start.13
  1077.8 387.8 %copy-start.1 = (bf16[256,2048]{1,0:T(8,128)(2,1)S(1)}, bf16[256,2048]{1,0:T(8,128)(2,1)}, u32[]{:S(2)}) copy-start(bf16[256,2048]{1,0:T(8,128)(2,1)} %param.10) | copy-start | bytes 3145732
  1077.8 387.8 %copy-start.28 = (f32[256]{0:T(256)S(1)}, f32[256]{0:T(256)}, u32[]{:S(2)}) copy-start(f32[256]{0:T(256)} %copy-done.27) | copy-start | bytes 3076
  1077.8 387.8 %copy-start.30 = (f32[256]{0:T(256)S(1)}, f32[256]{0:T(256)}, u32[]{:S(2)}) copy-start(f32[256]{0:T(256)} %copy-done.29) | copy-start | bytes 3076
  1137.3 330.3 %copy-start.2 = (f32[256,2048]{1,0:T(8,128)S(1)}, f32[256,2048]{1,0:T(8,128)}, u32[]{:S(2)}) copy-start(f32[256,2048]{1,0:T(8,128)} %get-tuple-element.55) | copy-start | bytes 6291460
Sparse Core Ops, SparseCore 0:
  9.9 30.4 all-gather.17
  42.6 80.7 all-gather.11
  125.2 26.2 all-gather.15
  153.3 27.7 all-gather.13
  182.8 28.0 all-gather.19
  218.3 144.6 reduce-scatter.11
  364.8 54.8 all-gather.25
  421.9 80.7 all-gather.21
  504.5 52.7 all-gather.23
  558.7 80.7 all-gather.29
  641.4 54.3 all-gather.27
  743.8 76.7 reduce-scatter.15
  822.9 77.2 reduce-scatter.13
  905.1 81.2 all-gather.31
  989.7 69.9 reduce-scatter.29
  1063.0 71.4 reduce-scatter.27
  1137.8 71.2 reduce-scatter.31
  1212.3 41.1 reduce-scatter.25
  1256.7 41.0 reduce-scatter.23
  1301.0 41.1 reduce-scatter.19
  1345.4 41.0 reduce-scatter.21
  1388.9 76.7 reduce-scatter.17
where the time goes:
time: 1490 us; the launch traced here: 1480 us
  waiting for transfers between devices  1130 us (76%)
  matrix products  241 us (16%)
  other arithmetic  68.2 us (5%)
  local copies, waits for them, and re-layouts  23.8 us (2%)
  between operations  15.3 us (1%)
    reduce_scatter x1, waiting for transfers between devices, per_device(): lax.psum_scatter(product(attended, full_output), 'row', scatter_dimension...  144 us
    all_gather x1, waiting for transfers between devices, per_device(): first_rows = lax.all_gather(normed_first, 'row', axis=0, tiled=True)  82.9 us
    all_gather x1, waiting for transfers between devices, per_device(): second_rows = lax.all_gather(normed_second, 'row', axis=0, tiled=True)  82.9 us
    reduce_scatter x1, waiting for transfers between devices, per_device(): lax.psum_scatter(product(activation, full_down).astype(jnp.bfloat16), 'ro...  77.8 us
    reduce_scatter x1, waiting for transfers between devices, per_device(): lax.psum_scatter((times_transpose(grad_query, back_query) + times_transpo...  77.3 us
    reduce_scatter x1, waiting for transfers between devices, per_device(): lax.psum_scatter(grad_down_w.astype(jnp.bfloat16), 'col', scatter_dimensi...  71.8 us
    all_gather x1, waiting for transfers between devices, per_device(): grad_rows = lax.all_gather(cotangent, 'row', axis=0, tiled=True)  67.7 us
    dot_general x7, matrix products, times_transpose(): lax.dot_general(left, right, (((1,), (1,)), ((), ())), preferred_element_...  67 us
  transfers between devices with their start and end apart: 22, of which 21 were waited for; matrix products, arithmetic and copies ran while one was open for 18% of the time, Pallas kernels for 0%

commit v1 on v0

--- a/solution.py
+++ b/solution.py
@@ -1,3 +1,4 @@
+import functools
 import math
 import jax
 import jax.numpy as jnp
@@ -9,6 +10,29 @@
 PIECE = 256
 EPSILON = 1e-05
 NEGATIVE = -1e30
+
+
+def compute_the_corner(buf, at_axis):
+    n_parts = lax.axis_size("row")
+    carry_in = range(n_parts)
+    current_value = map(lambda dev_j: (dev_j, (dev_j + 1) % n_parts), carry_in)
+    t1 = range(n_parts)
+    lanes = list(current_value)
+    r_now = map(lambda dev_j: (dev_j, (dev_j - 1) % n_parts), t1)
+    value_now, built = ([buf], [buf])
+    gallery = list(r_now)
+    for _ in range(n_parts // 2):
+        value_now.append(lax.ppermute(value_now[-1], "row", lanes))
+    for _ in tuple(range((n_parts - 1) // 2)):
+        built.append(lax.ppermute(built[-1], "row", gallery))
+    row_out = jnp.concatenate([*value_now[::-1], *built[1:]], at_axis)
+    side_arr = jnp.roll(
+        row_out, (lax.axis_index("row") - n_parts // 2) * buf.shape[at_axis], axis=at_axis
+    )
+    return side_arr
+
+
+lift_the_spot = functools.partial(compute_the_corner, at_axis=0)
 
 
 def product(left, right):
@@ -171,7 +195,7 @@
     output = (middle + ffn_sum).astype(jnp.bfloat16)
     back_query, back_key, back_value, back_output = (full_query, full_key, full_value, full_output)
     back_gate, back_up, back_down = (full_gate, full_up, full_down)
-    grad_rows = lax.all_gather(cotangent, "row", axis=0, tiled=True)
+    grad_rows = lift_the_spot(cotangent)
     grad_activation = times_transpose(grad_rows, back_down)
     sigma = jax.nn.sigmoid(gate_lin)
     grad_gate = (grad_activation * up_lin * sigma * (1.0 + gate_lin * (1.0 - sigma))).astype(

time: 1490 us -> 1420 us (0.953)
  waiting for transfers between devices: 1130 us -> 1030 us
  local copies, waits for them, and re-layouts: 23.8 us -> 39.8 us
    ppermute x0 -> x3, waiting for transfers between devices: none -> 80.9 us  [the longest x2 49.5 us: compute_the_corner(): value_now.append(lax.ppermute(value_now[-1], 'row', lanes))]
    reduce_scatter x1, waiting for transfers between devices: 71.8 us -> 0.02 us  [per_device(): lax.psum_scatter(grad_down_w.astype(jnp.bfloat16), 'col', scatter_dimensi...]
    all_gather x1 -> x0, waiting for transfers between devices: 67.7 us -> none  [per_device(): grad_rows = lax.all_gather(cotangent, 'row', axis=0, tiled=True)]
    reduce_scatter x1, waiting for transfers between devices: 0.02 us -> 56.4 us  [per_device(): lax.psum_scatter(grad_up_w.astype(jnp.bfloat16), 'col', scatter_dimension...]
    all_gather x1, waiting for transfers between devices: 51.1 us -> 0.01 us  [per_device(): lax.all_gather(w_up, 'col', axis=0, tiled=True)]
    all_gather x1, waiting for transfers between devices: 82.9 us -> 40.4 us  [per_device(): second_rows = lax.all_gather(normed_second, 'row', axis=0, tiled=True)]
    reduce_scatter x1, waiting for transfers between devices: 56.7 us -> 72.1 us  [per_device(): lax.psum_scatter(grad_gate_w.astype(jnp.bfloat16), 'col', scatter_dimensi...]
    unnamed x78 -> x85, local copies, waits for them, and re-layouts: 16.2 us -> 30 us
  transfers between devices with their start and end apart: 22 -> 24, of which waited for: 21 -> 22; matrix products, arithmetic and copies ran while one was open for 18% -> 20% of each run, Pallas kernels for 0% -> 0%
where the time goes in v1:
time: 1420 us; the launch traced here: 1410 us
  waiting for transfers between devices  1030 us (73%)
  matrix products  241 us (17%)
  other arithmetic  68.3 us (5%)
  local copies, waits for them, and re-layouts  39.8 us (3%)
  between operations  15.3 us (1%)
    reduce_scatter x1, waiting for transfers between devices, per_device(): lax.psum_scatter(product(attended, full_output), 'row', scatter_dimension...  144 us
    all_gather x1, waiting for transfers between devices, per_device(): first_rows = lax.all_gather(normed_first, 'row', axis=0, tiled=True)  82.9 us
    reduce_scatter x1, waiting for transfers between devices, per_device(): lax.psum_scatter(product(activation, full_down).astype(jnp.bfloat16), 'ro...  77.6 us
    reduce_scatter x1, waiting for transfers between devices, per_device(): lax.psum_scatter((times_transpose(grad_query, back_query) + times_transpo...  77.3 us
    reduce_scatter x1, waiting for transfers between devices, per_device(): lax.psum_scatter(grad_gate_w.astype(jnp.bfloat16), 'col', scatter_dimensi...  72.1 us
    dot_general x7, matrix products, times_transpose(): lax.dot_general(left, right, (((1,), (1,)), ((), ())), preferred_element_...  67.1 us
    dot_general x7, matrix products, product(): return jnp.dot(left, right, preferred_element_type=jnp.float32)  65.7 us
    dot_general x7, matrix products, contract_rows(): lax.dot_general(left, right, (((0,), (0,)), ((), ())), preferred_element_...  64.7 us
  transfers between devices with their start and end apart: 24, of which 22 were waited for; matrix products, arithmetic and copies ran while one was open for 20% of the time, Pallas kernels for 0%

profile of v1, /device:TPU:0, one launch (start us, length us, event | category | flops | bytes accessed | tf_op | source)
XLA Modules:
  0.0 1405.1 jit_solution(4308192044159121640)
XLA Ops:
  11.7 2.5 fusion.13
  18.2 2.6 copy.49
  22.7 17.7 %all-gather.17.cloned.1.call-done = bf16[2048,512]{1,0:T(8,128)(2,1)} async-done(((bf16[256,512]{1,0:T(8,128)(2,1)}), bf16[2048,512]{1,0:T(8,128)(2,1)}) %all-gather.17.cloned.1.call-update) | async-done | bytes 2097168 | tf_op jit(solution)/shard_map/all_gather | solution.py:157
  40.4 82.9 %all-gather.11.cloned.1.call-done = bf16[1024,2048]{1,0:T(8,128)(2,1)} async-done(((bf16[256,2048]{1,0:T(8,128)(2,1)}), bf16[1024,2048]{1,0:T(8,128)(2,1)}) %all-gather.11.cloned.1.call-update) | async-done | bytes 4194320 | tf_op jit(solution)/shard_map/all_gather | solution.py:168
  123.3 5.2 fusion.46
  132.0 3.2 copy.78
  135.2 16.4 %all-gather.15.cloned.1.call-done = bf16[2048,512]{1,0:T(8,128)(2,1)} async-done(((bf16[256,512]{1,0:T(8,128)(2,1)}), bf16[2048,512]{1,0:T(8,128)(2,1)}) %all-gather.15.cloned.1.call-update) | async-done | bytes 2097168 | tf_op jit(solution)/shard_map/all_gather | solution.py:156
  151.5 5.2 fusion.45
  158.3 3.2 copy.77
  161.5 3.2 copy.76
  164.6 4.0 fusion.28
  170.7 8.5 fusion.44
  181.1 5.2 convolution_convert_fusion.9
  186.3 8.6 fusion
  195.6 7.6 fusion.24
  203.2 7.8 all-gather.19.cloned.1.call-done
  210.9 7.2 fusion.47
  219.0 144.0 %reduce-scatter.12.cloned.1.call-done = f32[256,2048]{1,0:T(8,128)} async-done(((f32[1024,2048]{1,0:T(8,128)}), f32[256,2048]{1,0:T(8,128)}) %reduce-scatter.12.cloned.1.call-update) | async-done | bytes 2097168 | tf_op jit(solution)/shard_map/reduce_scatter | solution.py:183
  369.0 25.3 %collective-permute-done = bf16[256,2048]{1,0:T(8,128)(2,1)} collective-permute-done((bf16[256,2048]{1,0:T(8,128)(2,1)S(1)}, bf16[256,2048]{1,0:T(8,128)(2,1)}, u32[]{:S(2)}, u32[]{:S(2)}) %collective-permute-start) | collective-permute-done | bytes 1048608 | tf_op jit(solution)/shard_map/ppermute | solution.py:25
  394.4 4.0 collective-permute-start.2
  398.4 24.1 %collective-permute-done.1 = bf16[256,2048]{1,0:T(8,128)(2,1)} collective-permute-done((bf16[256,2048]{1,0:T(8,128)(2,1)}, bf16[256,2048]{1,0:T(8,128)(2,1)}, u32[]{:S(2)}, u32[]{:S(2)}) %collective-permute-start.1) | collective-permute-done | bytes 1048608 | tf_op jit(solution)/shard_map/ppermute | solution.py:25
  428.2 31.4 %collective-permute-done.2 = bf16[256,2048]{1,0:T(8,128)(2,1)} collective-permute-done((bf16[256,2048]{1,0:T(8,128)(2,1)S(1)}, bf16[256,2048]{1,0:T(8,128)(2,1)}, u32[]{:S(2)}, u32[]{:S(2)}) %collective-permute-start.2) | collective-permute-done | bytes 1048608 | tf_op jit(solution)/shard_map/ppermute | solution.py:27
  459.6 2.3 constant_dynamic-update-slice_fusion.4
  461.9 2.3 constant_dynamic-update-slice_fusion.3
  470.0 40.4 %all-gather.21.cloned.1.call-done = bf16[1024,2048]{1,0:T(8,128)(2,1)} async-done(((bf16[256,2048]{1,0:T(8,128)(2,1)}), bf16[1024,2048]{1,0:T(8,128)(2,1)}) %all-gather.21.cloned.1.call-update) | async-done | bytes 4194320 | tf_op jit(solution)/shard_map/all_gather | solution.py:188
  510.4 14.5 %fusion.49 = f32[1024,2048]{1,0:T(8,128)} fusion(bf16[1024,2048]{1,0:T(8,128)(2,1)} %all-gather.21.cloned.1.call-done, bf16[2048,2048]{1,0:T(8,128)(2,1)} %all-gather.25.cloned.1.call-done), kind=kOutput, calls=%fused_computation.116 | convolution fusion | flops 8589934592 | bytes 20971520 | tf_op jit(solution)/shard_map/dot_general | solution.py:39
  524.9 40.5 %all-gather.23.cloned.1.call-done = bf16[2048,2048]{1,0:T(8,128)(2,1)} async-done(((bf16[256,2048]{1,0:T(8,128)(2,1)}), bf16[2048,2048]{1,0:T(8,128)(2,1)}) %all-gather.23.cloned.1.call-update) | async-done | bytes 8388624 | tf_op jit(solution)/shard_map/all_gather | solution.py:160
  565.4 14.4 %fusion.48 = f32[1024,2048]{1,0:T(8,128)} fusion(bf16[1024,2048]{1,0:T(8,128)(2,1)} %all-gather.21.cloned.1.call-done, bf16[2048,2048]{1,0:T(8,128)(2,1)} %all-gather.23.cloned.1.call-done), kind=kOutput, calls=%fused_computation.115 | convolution fusion | flops 8589934592 | bytes 20971520 | tf_op jit(solution)/shard_map/dot_general | solution.py:39
  579.8 43.2 %all-gather.27.cloned.1.call-done = bf16[2048,2048]{1,0:T(8,128)(2,1)} async-done(((bf16[2048,256]{1,0:T(8,128)(2,1)}), bf16[2048,2048]{1,0:T(8,128)(2,1)}) %all-gather.27.cloned.1.call-update) | async-done | bytes 8388624 | tf_op jit(solution)/shard_map/all_gather | solution.py:162
  623.0 21.9 %multiply_convert_fusion.1 = (bf16[1024,2048]{1,0:T(8,128)(2,1)}, bf16[1024,2048]{1,0:T(8,128)(2,1)}, bf16[1024,2048]{1,0:T(8,128)(2,1)}) fusion(f32[1024,2048]{1,0:T(8,128)} %fusion.48, f32[1024,2048]{1,0:T(8,128)} %fusion.49, bf16[2048,2048]{1,0:T(8,128)(2,1)} %all-gather.27.cloned.1.call-done, bf16[2048,2048]{1,0:T(8,128)(2,1)} %constant_dynamic-update-slice_fusion, ...), kind=kOutput, calls=%fused_computation.12 | convolution fusion | flops 8623489024 | bytes 41943044 | tf_op jit(solution)/shard_map/dot_general | solution.py:49
  644.9 13.1 fusion.50
  658.0 12.9 add_convert_fusion.1
  671.0 13.9 convolution_convert_fusion.3
  685.2 62.7 %reduce-scatter.16.cloned.1.call-done = bf16[256,2048]{1,0:T(8,128)(2,1)} async-done(((bf16[1024,2048]{1,0:T(8,128)(2,1)}), bf16[256,2048]{1,0:T(8,128)(2,1)}) %reduce-scatter.16.cloned.1.call-update) | async-done | bytes 1048592 | tf_op jit(solution)/shard_map/reduce_scatter | solution.py:205
  749.8 77.6 %reduce-scatter.14.cloned.1.call-done = bf16[256,2048]{1,0:T(8,128)(2,1)} async-done(((bf16[1024,2048]{1,0:T(8,128)(2,1)}), bf16[256,2048]{1,0:T(8,128)(2,1)}) %reduce-scatter.14.cloned.1.call-update) | async-done | bytes 1048592 | tf_op jit(solution)/shard_map/reduce_scatter | solution.py:192
  827.4 4.6 fusion.39
  832.1 14.1 %convolution_convert_fusion = bf16[2048,2048]{1,0:T(8,128)(2,1)} fusion(bf16[1024,2048]{1,0:T(8,128)(2,1)} %get-tuple-element.70, bf16[2048,2048]{1,0:T(8,128)(2,1)} %constant_dynamic-update-slice_fusion, s32[]{:T(128)S(6)} %select_n.22), kind=kOutput, calls=%fused_computation.18 | convolution fusion | flops 8594128896 | bytes 16777220 | tf_op jit(solution)/shard_map/dot_general | solution.py:43
  846.2 14.1 %convolution_convert_fusion.1 = bf16[2048,2048]{1,0:T(8,128)(2,1)} fusion(bf16[1024,2048]{1,0:T(8,128)(2,1)} %all-gather.21.cloned.1.call-done, bf16[1024,2048]{1,0:T(8,128)(2,1)} %get-tuple-element.68), kind=kOutput, calls=%fused_computation.19 | convolution fusion | flops 8594128896 | bytes 16777216 | tf_op jit(solution)/shard_map/dot_general | solution.py:43
  860.6 14.1 %convolution_convert_fusion.2 = bf16[2048,2048]{1,0:T(8,128)(2,1)} fusion(bf16[1024,2048]{1,0:T(8,128)(2,1)} %all-gather.21.cloned.1.call-done, bf16[1024,2048]{1,0:T(8,128)(2,1)} %get-tuple-element.69), kind=kOutput, calls=%fused_computation.20 | convolution fusion | flops 8594128896 | bytes 16777216 | tf_op jit(solution)/shard_map/dot_general | solution.py:43
  875.5 38.0 %all-gather.29.cloned.1.call-done = bf16[1024,2048]{1,0:T(8,128)(2,1)} async-done(((bf16[256,2048]{1,0:T(8,128)(2,1)}), bf16[1024,2048]{1,0:T(8,128)(2,1)}) %all-gather.29.cloned.1.call-update) | async-done | bytes 4194320 | tf_op jit(solution)/shard_map/all_gather | solution.py:214
  913.5 5.9 convolution_convert_fusion.4
  919.8 6.1 convolution_convert_fusion.8
  925.9 10.8 fusion.25
  937.7 3.9 convolution_convert_fusion.5
  941.5 11.0 multiply_reduce_fusion
  952.8 12.6 multiply_convert_fusion
  965.4 3.4 multiply_bitcast_fusion.1
  968.9 2.4 multiply_bitcast_fusion
  974.6 6.3 convolution_convert_fusion.7
  982.3 6.4 convolution_convert_fusion.6
  988.8 4.5 fusion.52
  993.3 2.4 fusion.51
  995.7 6.3 add_convert_fusion
  1002.1 2.9 convert_element_type.184
  1005.0 56.4 %reduce-scatter.30.cloned.1.call-done = bf16[256,2048]{1,0:T(8,128)(2,1)} async-done(((bf16[2048,2048]{1,0:T(8,128)(2,1)}), bf16[256,2048]{1,0:T(8,128)(2,1)}) %reduce-scatter.30.cloned.1.call-update) | async-done | bytes 1048592 | tf_op jit(solution)/shard_map/reduce_scatter | solution.py:256
  1061.4 2.8 convert_element_type.182
  1064.2 72.1 %reduce-scatter.28.cloned.1.call-done = bf16[256,2048]{1,0:T(8,128)(2,1)} async-done(((bf16[2048,2048]{1,0:T(8,128)(2,1)}), bf16[256,2048]{1,0:T(8,128)(2,1)}) %reduce-scatter.28.cloned.1.call-update) | async-done | bytes 1048592 | tf_op jit(solution)/shard_map/reduce_scatter | solution.py:253
  1136.2 2.8 convert_element_type.180
  1139.0 41.5 %reduce-scatter.26.cloned.1.call-done = bf16[512,256]{1,0:T(8,128)(2,1)} async-done(((bf16[512,2048]{1,0:T(8,128)(2,1)}), bf16[512,256]{1,0:T(8,128)(2,1)}) %reduce-scatter.26.cloned.1.call-update) | async-done | bytes 262160 | tf_op jit(solution)/shard_map/reduce_scatter | solution.py:250
  1182.3 42.5 %reduce-scatter.24.cloned.1.call-done = bf16[256,512]{1,0:T(8,128)(2,1)} async-done(((bf16[2048,512]{1,0:T(8,128)(2,1)}), bf16[256,512]{1,0:T(8,128)(2,1)}) %reduce-scatter.24.cloned.1.call-update) | async-done | bytes 262160 | tf_op jit(solution)/shard_map/reduce_scatter | solution.py:247
  1226.6 42.6 %reduce-scatter.20.cloned.1.call-done = bf16[256,512]{1,0:T(8,128)(2,1)} async-done(((bf16[2048,512]{1,0:T(8,128)(2,1)}), bf16[256,512]{1,0:T(8,128)(2,1)}) %reduce-scatter.20.cloned.1.call-update) | async-done | bytes 262160 | tf_op jit(solution)/shard_map/reduce_scatter | solution.py:241
  1271.0 42.5 %reduce-scatter.22.cloned.1.call-done = bf16[256,512]{1,0:T(8,128)(2,1)} async-done(((bf16[2048,512]{1,0:T(8,128)(2,1)}), bf16[256,512]{1,0:T(8,128)(2,1)}) %reduce-scatter.22.cloned.1.call-update) | async-done | bytes 262160 | tf_op jit(solution)/shard_map/reduce_scatter | solution.py:244
  1315.3 77.3 %reduce-scatter.18.cloned.1.call-done = bf16[256,2048]{1,0:T(8,128)(2,1)} async-done(((bf16[1024,2048]{1,0:T(8,128)(2,1)}), bf16[256,2048]{1,0:T(8,128)(2,1)}) %reduce-scatter.18.cloned.1.call-update) | async-done | bytes 1048592 | tf_op jit(solution)/shard_map/reduce_scatter | solution.py:222
  1394.6 3.3 fusion.16
  (160 shorter events, 56.8 us)
Async XLA Ops:
  7.2 9.0 copy-start.31
  7.2 33.2 %all-gather.17.cloned.1.call-start = ((), (), s32[]{:S(2)}) async-start(), calls=%async_computation.14 | async-start | bytes 2359296 | tf_op jit(solution)/shard_map/all_gather | solution.py:157
  7.9 115.4 %all-gather.11.cloned.1.call-start = ((), (), s32[]{:S(2)}) async-start(), calls=%async_computation.11 | async-start | bytes 5242880 | tf_op jit(solution)/shard_map/all_gather | solution.py:168
  9.4 1.7 copy-start.27
  11.1 0.6 copy-start.29
  14.2 137.3 %all-gather.15.cloned.1.call-start = ((), (), s32[]{:S(2)}) async-start(), calls=%async_computation.13 | async-start | bytes 2359296 | tf_op jit(solution)/shard_map/all_gather | solution.py:156
  15.0 166.1 %all-gather.13.cloned.1.call-start = ((), (), s32[]{:S(2)}) async-start(), calls=%async_computation.12 | async-start | bytes 2359296 | tf_op jit(solution)/shard_map/all_gather | solution.py:158
  15.5 195.4 %all-gather.19.cloned.1.call-start = ((), (), s32[]{:S(2)}) async-start(), calls=%async_computation.15 | async-start | bytes 2359296 | tf_op jit(solution)/shard_map/all_gather | solution.py:159
  16.1 346.8 %reduce-scatter.12.cloned.1.call-start = ((), (), s32[]{:S(2)}) async-start(), calls=%async_computation.16 | async-start | bytes 10485760 | tf_op jit(solution)/shard_map/reduce_scatter | solution.py:183
  22.7 141.9 %copy-start.4 = (f32[1024,64]{1,0:T(8,128)}, f32[1024,64]{1,0:T(8,128)S(1)}, u32[]{:S(2)}) copy-start(f32[1024,64]{1,0:T(8,128)S(1)} %get-tuple-element.88) | copy-start | bytes 786436
  22.7 141.9 %copy-start.6 = (f32[1024,64]{1,0:T(8,128)}, f32[1024,64]{1,0:T(8,128)S(1)}, u32[]{:S(2)}) copy-start(f32[1024,64]{1,0:T(8,128)S(1)} %get-tuple-element.89) | copy-start | bytes 786436
  164.6 6.0 copy-start.16
  168.7 1.0 copy-start.8
  168.7 1.3 copy-start.10
  168.7 1.6 copy-start.19
  168.7 2.0 copy-start.21
  179.2 15.8 %copy-start.23 = (f32[4,1024]{1,0:T(4,128)}, f32[4,1024]{1,0:T(4,128)S(1)}, u32[]{:S(2)}) copy-start(f32[4,1024]{1,0:T(4,128)S(1)} %get-tuple-element.90) | copy-start | bytes 49156
  186.3 8.7 copy-start.14
  195.0 0.6 copy-start.25
  203.2 15.0 %copy-start.34 = (bf16[4,128,1024]{2,1,0:T(8,128)(2,1)}, bf16[4,128,1024]{2,1,0:T(8,128)(2,1)S(1)}, u32[]{:S(2)}) copy-start(bf16[4,128,1024]{2,1,0:T(8,128)(2,1)S(1)} %fusion.24) | copy-start | bytes 3145732
  218.2 144.8 %copy-start = (bf16[256,2048]{1,0:T(8,128)(2,1)S(1)}, bf16[256,2048]{1,0:T(8,128)(2,1)}, u32[]{:S(2)}) copy-start(bf16[256,2048]{1,0:T(8,128)(2,1)} %param.10) | copy-start | bytes 3145732
  218.2 251.8 %all-gather.25.cloned.1.call-start = ((), (), s32[]{:S(2)}) async-start(), calls=%async_computation.19 | async-start | bytes 9437184 | tf_op jit(solution)/shard_map/all_gather | solution.py:161
  218.9 291.4 %all-gather.21.cloned.1.call-start = ((), (), s32[]{:S(2)}) async-start(), calls=%async_computation.17 | async-start | bytes 5242880 | tf_op jit(solution)/shard_map/all_gather | solution.py:188
  364.8 3.0 copy-start.2
  366.5 198.9 %all-gather.23.cloned.1.call-start = ((), (), s32[]{:S(2)}) async-start(), calls=%async_computation.18 | async-start | bytes 9437184 | tf_op jit(solution)/shard_map/all_gather | solution.py:160
  367.2 255.8 %all-gather.27.cloned.1.call-start = ((), (), s32[]{:S(2)}) async-start(), calls=%async_computation.20 | async-start | bytes 9437184 | tf_op jit(solution)/shard_map/all_gather | solution.py:162
  367.8 380.1 %reduce-scatter.16.cloned.1.call-start = ((), (), s32[]{:S(2)}) async-start(), calls=%async_computation.22 | async-start | bytes 5242880 | tf_op jit(solution)/shard_map/reduce_scatter | solution.py:205
  367.9 26.5 %collective-permute-start = (bf16[256,2048]{1,0:T(8,128)(2,1)S(1)}, bf16[256,2048]{1,0:T(8,128)(2,1)}, u32[]{:S(2)}, u32[]{:S(2)}) collective-permute-start(bf16[256,2048]{1,0:T(8,128)(2,1)S(1)} %copy-done.2), channel_id=1, source_target_pairs={{0,8},{8,16},{16,24},{24,0},{1,9},{9,17},{17,25},{25,1},{2,10},{10... | collective-permute-start | bytes 3145736 | tf_op jit(solution)/shard_map/ppermute | solution.py:25
  394.3 28.2 %collective-permute-start.1 = (bf16[256,2048]{1,0:T(8,128)(2,1)}, bf16[256,2048]{1,0:T(8,128)(2,1)}, u32[]{:S(2)}, u32[]{:S(2)}) collective-permute-start(bf16[256,2048]{1,0:T(8,128)(2,1)} %collective-permute-done), channel_id=1, source_target_pairs={{0,8},{8,16},{16,24},{24,0},{1,9},{9,17},{17,25},{25,1},{2,10},{10... | collective-permute-start | bytes 3145736 | tf_op jit(solution)/shard_map/ppermute | solution.py:25
  394.4 65.2 %collective-permute-start.2 = (bf16[256,2048]{1,0:T(8,128)(2,1)S(1)}, bf16[256,2048]{1,0:T(8,128)(2,1)}, u32[]{:S(2)}, u32[]{:S(2)}) collective-permute-start(bf16[256,2048]{1,0:T(8,128)(2,1)S(1)} %copy-done.2), channel_id=1, source_target_pairs={{0,24},{8,0},{16,8},{24,16},{1,25},{9,1},{17,9},{25,17},{2,26},{10... | collective-permute-start | bytes 3145736 | tf_op jit(solution)/shard_map/ppermute | solution.py:27
  644.9 13.2 copy-start.36
  671.0 156.4 %reduce-scatter.14.cloned.1.call-start = ((), (), s32[]{:S(2)}) async-start(), calls=%async_computation.21 | async-start | bytes 5242880 | tf_op jit(solution)/shard_map/reduce_scatter | solution.py:192
  684.9 228.5 %all-gather.29.cloned.1.call-start = ((), (), s32[]{:S(2)}) async-start(), calls=%async_computation.23 | async-start | bytes 5242880 | tf_op jit(solution)/shard_map/all_gather | solution.py:214
  832.1 170.0 %reduce-scatter.32.cloned.1.call-start = ((), (), s32[]{:S(2)}) async-start(), calls=%async_computation.31 | async-start | bytes 9437184 | tf_op jit(solution)/shard_map/reduce_scatter | solution.py:259
  846.2 215.2 %reduce-scatter.30.cloned.1.call-start = ((), (), s32[]{:S(2)}) async-start(), calls=%async_computation.30 | async-start | bytes 9437184 | tf_op jit(solution)/shard_map/reduce_scatter | solution.py:256
  860.4 275.9 %reduce-scatter.28.cloned.1.call-start = ((), (), s32[]{:S(2)}) async-start(), calls=%async_computation.29 | async-start | bytes 9437184 | tf_op jit(solution)/shard_map/reduce_scatter | solution.py:253
  874.7 0.7 copy-start.24
  874.7 0.7 copy-start.26
  874.7 38.8 %copy-start.35 = (bf16[4,128,1024]{2,1,0:T(8,128)(2,1)S(1)}, bf16[4,128,1024]{2,1,0:T(8,128)(2,1)}, u32[]{:S(2)}) copy-start(bf16[4,128,1024]{2,1,0:T(8,128)(2,1)} %copy-done.34) | copy-start | bytes 3145732
  874.7 305.8 %reduce-scatter.26.cloned.1.call-start = ((), (), s32[]{:S(2)}) async-start(), calls=%async_computation.28 | async-start | bytes 2359296 | tf_op jit(solution)/shard_map/reduce_scatter | solution.py:250
  919.4 305.4 %reduce-scatter.24.cloned.1.call-start = ((), (), s32[]{:S(2)}) async-start(), calls=%async_computation.27 | async-start | bytes 2359296 | tf_op jit(solution)/shard_map/reduce_scatter | solution.py:247
  925.9 11.8 copy-start.32
  936.7 1.0 copy-start.12
  937.6 3.9 copy-start.15
  952.5 316.7 %reduce-scatter.20.cloned.1.call-start = ((), (), s32[]{:S(2)}) async-start(), calls=%async_computation.25 | async-start | bytes 2359296 | tf_op jit(solution)/shard_map/reduce_scatter | solution.py:241
  952.7 12.6 copy-start.9
  952.8 12.6 copy-start.11
  965.4 3.4 copy-start.20
  965.4 3.4 copy-start.22
  968.8 2.4 copy-start.5
  968.8 2.4 copy-start.7
  980.9 332.6 %reduce-scatter.22.cloned.1.call-start = ((), (), s32[]{:S(2)}) async-start(), calls=%async_computation.26 | async-start | bytes 2359296 | tf_op jit(solution)/shard_map/reduce_scatter | solution.py:244
  982.3 6.4 copy-start.18
  988.8 4.5 copy-start.17
  988.8 403.9 %reduce-scatter.18.cloned.1.call-start = ((), (), s32[]{:S(2)}) async-start(), calls=%async_computation.24 | async-start | bytes 5242880 | tf_op jit(solution)/shard_map/reduce_scatter | solution.py:222
  988.8 4.5 copy-start.33
  993.3 2.4 copy-start.13
  1005.0 387.7 %copy-start.1 = (bf16[256,2048]{1,0:T(8,128)(2,1)S(1)}, bf16[256,2048]{1,0:T(8,128)(2,1)}, u32[]{:S(2)}) copy-start(bf16[256,2048]{1,0:T(8,128)(2,1)} %param.10) | copy-start | bytes 3145732
  1005.0 387.7 %copy-start.28 = (f32[256]{0:T(256)S(1)}, f32[256]{0:T(256)}, u32[]{:S(2)}) copy-start(f32[256]{0:T(256)} %copy-done.27) | copy-start | bytes 3076
  1005.0 387.7 %copy-start.30 = (f32[256]{0:T(256)S(1)}, f32[256]{0:T(256)}, u32[]{:S(2)}) copy-start(f32[256]{0:T(256)} %copy-done.29) | copy-start | bytes 3076
  1064.2 330.4 %copy-start.3 = (f32[256,2048]{1,0:T(8,128)S(1)}, f32[256,2048]{1,0:T(8,128)}, u32[]{:S(2)}) copy-start(f32[256,2048]{1,0:T(8,128)} %get-tuple-element.55) | copy-start | bytes 6291460
Sparse Core Ops, SparseCore 0:
  9.9 30.4 all-gather.16
  42.6 80.7 all-gather.10
  125.2 26.2 all-gather.14
  153.3 27.7 all-gather.12
  182.8 28.0 all-gather.18
  218.3 144.6 reduce-scatter.11
  364.8 54.8 all-gather.24
  421.9 88.4 all-gather.20
  512.3 53.0 all-gather.22
  567.1 55.8 all-gather.26
  671.1 76.7 reduce-scatter.15
  750.1 77.2 reduce-scatter.13
  832.2 81.2 all-gather.28
  916.8 69.7 reduce-scatter.31
  989.9 71.4 reduce-scatter.29
  1064.7 71.4 reduce-scatter.27
  1139.4 41.1 reduce-scatter.25
  1183.7 41.0 reduce-scatter.23
  1228.1 41.1 reduce-scatter.19
  1272.4 41.1 reduce-scatter.21
  1315.8 76.7 reduce-scatter.17
